TPU v7x, 512 devices: a whole 4x8x8 slice. The times are simulated.
512 devices in a mesh: seq: 64 (over z, x, y_lo), tensor: 8 (over y_hi, core).
Axes of the slice: x: 4, y: 8 (y_hi: 4, y_lo: 2; y = y_hi * 2 + y_lo), z: 8, core: 2. Of those that a mesh axis runs over, the one named last changes fastest.
Arguments:
- hidden_in: bfloat16 [8192, 2560], P('seq', 'tensor'), may hold values from -6 to 6
- norm_gain: float32 [2560], replicated, may hold values from 0.1 to 1.9
- w_query: bfloat16 [2560, 2048], P(None, 'tensor'), may hold values from -0.125 to 0.125
- w_key: bfloat16 [2560, 1024], P(None, 'tensor'), may hold values from -0.125 to 0.125
- w_value: bfloat16 [2560, 1024], P(None, 'tensor'), may hold values from -0.125 to 0.125
- w_out: bfloat16 [2048, 2560], P('tensor'), may hold values from -0.125 to 0.125
- q_gain: float32 [128], replicated, may hold values from 0.1 to 1.9
- k_gain: float32 [128], replicated, may hold values from 0.1 to 1.9
- lengths: int32 [16], replicated, may hold values from 1 to 6144, 8192 in all
Outputs:
- attn_out: bfloat16 [8192, 2560], P(('seq', 'tensor'))
- key_cache: bfloat16 [8192, 1024], P('seq', 'tensor')
- value_cache: bfloat16 [8192, 1024], P('seq', 'tensor')
Inputs may be any that keep to these rules, and one draw needn't show every extreme that they name: The lengths sum to 8192 and the largest is exactly 6144.
All inputs are finite; a program needn't handle non-finite values.
Results may differ from a plain program's by a relative error of at most 0.015.
Values may be sent and summed in bfloat16 or wider, within the bound.
No kernel may reach another device: no remote copies, remote signals or barrier semaphores. Data moves between devices by JAX's collectives and lax.ppermute only.
A program may use at most 64 MiB of HBM per device.

v0:
```python
import math
import jax
import jax.numpy as jnp
from jax import lax
from jax.sharding import Mesh
from jax.sharding import PartitionSpec as P

rope_base = 1000000.0
norm_eps = 1e-06
masked = -1e30
max_len = 6144
SEQ = ("z", "x", "ylo")
TEN = ("yhi", "core")


def prompt_starts(lengths, token_pos):
    ends = jnp.cumsum(lengths)
    starts = ends - lengths
    before = (ends[None, :] <= token_pos[:, None]).astype(jnp.int32)
    segment = jnp.sum(before, axis=1)
    onehot = segment[:, None] == jnp.arange(lengths.shape[0], dtype=jnp.int32)[None, :]
    return jnp.sum(jnp.where(onehot, starts[None, :], 0), axis=1)


def head_norm_rope(values, gain, rel_pos):
    width = values.shape[-1]
    half = width // 2
    mean_sq = jnp.mean(values * values, axis=-1, keepdims=True)
    normed = values * lax.rsqrt(mean_sq + norm_eps) * gain
    freq = rope_base ** (-jnp.arange(half, dtype=jnp.float32) * 2.0 / width)
    angle = rel_pos.astype(jnp.float32)[:, None] * freq[None, :]
    cosine = jnp.cos(angle)[:, None, :]
    sine = jnp.sin(angle)[:, None, :]
    first = normed[..., :half]
    second = normed[..., half:]
    return jnp.concatenate(
        [first * cosine - second * sine, second * cosine + first * sine], axis=-1
    )


def ring_pairs(n, k, forward, needed):
    out = []
    for src in range(n):
        if forward:
            start, dst = ((src - (k - 1)) % n, (src + 1) % n)
            reach = [(start + j) % n for j in range(k, n // 2 + 1)]
        else:
            start, dst = ((src + (k - 1)) % n, (src - 1) % n)
            reach = [(start - j) % n for j in range(k, n // 2 + 1)]
        if any((needed(start, d) for d in reach)):
            out.append((src, dst))
    return out


def ring_gather(piece, inner, name, stride, needed=lambda p, d: True):
    n = lax.axis_size(name)
    c = lax.axis_index(name)
    pieces, ids = ([piece], [c * stride + inner])
    a = b = piece
    if n % 2 == 0 and n >= 4:
        last = n // 2 - 1
        m = piece.shape[0]
        half = m // 2 if m % 2 == 0 else m
        for s in range(1, last + 1):
            if s == last:
                far = (c + n // 2) % n * stride
                ahead = [
                    (src, (src + 2) % n)
                    for src in range(n)
                    if needed((src - (last - 1)) % n, (src + 2) % n)
                ]
                pieces.append(lax.ppermute(a[:half], name, ahead))
                ids.append(far + inner[:half])
                if half < m:
                    behind = [
                        (src, (src - 2) % n)
                        for src in range(n)
                        if needed((src + (last - 1)) % n, (src - 2) % n)
                    ]
                    pieces.append(lax.ppermute(b[half:], name, behind))
                    ids.append(far + inner[half:])
            a = lax.ppermute(a, name, ring_pairs(n, s, True, needed))
            b = lax.ppermute(b, name, ring_pairs(n, s, False, needed))
            pieces += [a, b]
            ids += [(c - s) % n * stride + inner, (c + s) % n * stride + inner]
        return (jnp.concatenate(pieces, axis=0), jnp.concatenate(ids, axis=0))
    for s in range(1, (n - 1) // 2 + 1):
        a = lax.ppermute(a, name, ring_pairs(n, s, True, needed))
        b = lax.ppermute(b, name, ring_pairs(n, s, False, needed))
        pieces += [a, b]
        ids += [(c - s) % n * stride + inner, (c + s) % n * stride + inner]
    if n % 2 == 0:
        s = n // 2
        far = (c + s) % n * stride
        m = piece.shape[0]
        if m % 2 == 0:
            pieces += [
                lax.ppermute(a[: m // 2], name, ring_pairs(n, s, True, needed)),
                lax.ppermute(b[m // 2 :], name, ring_pairs(n, s, False, needed)),
            ]
            ids += [far + inner[: m // 2], far + inner[m // 2 :]]
        else:
            pieces += [lax.ppermute(a, name, ring_pairs(n, s, True, needed))]
            ids += [far + inner]
    return (jnp.concatenate(pieces, axis=0), jnp.concatenate(ids, axis=0))


def on_device(hidden_in, norm_gain, w_query, w_key, w_value, w_out, q_gain, k_gain, lengths):
    tokens = hidden_in.shape[0]
    width = w_query.shape[0]
    head_dim = q_gain.shape[0]
    q_cols = w_query.shape[1]
    kv_cols = w_key.shape[1]
    kv_local = kv_cols // head_dim
    group = q_cols // kv_cols
    combined = jnp.concatenate([w_query, w_key, w_value], axis=1)
    piece = lax.all_gather(hidden_in, TEN, axis=1, tiled=True)
    wide = piece.astype(jnp.float32)
    scaled = (wide * norm_gain[None, :]).astype(jnp.bfloat16)
    acc = jnp.dot(scaled, combined, preferred_element_type=jnp.float32)
    sumsq = jnp.sum(wide * wide, axis=1)
    proj = acc * lax.rsqrt(sumsq / width + norm_eps)[:, None]
    block_index = lax.axis_index(SEQ)
    token_pos = block_index * tokens + jnp.arange(tokens, dtype=jnp.int32)
    seg_start = prompt_starts(lengths, token_pos)
    rel_pos = token_pos - seg_start
    queries = head_norm_rope(
        proj[:, :q_cols].reshape(tokens, kv_local * group, head_dim), q_gain, rel_pos
    ).astype(jnp.bfloat16)
    keys = head_norm_rope(
        proj[:, q_cols : q_cols + kv_cols].reshape(tokens, kv_local, head_dim), k_gain, rel_pos
    ).astype(jnp.bfloat16)
    key_flat = keys.reshape(tokens, kv_cols)
    value_flat = proj[:, q_cols + kv_cols :].astype(jnp.bfloat16)
    nx, nlo = (lax.axis_size("x"), lax.axis_size("ylo"))
    piece = jnp.concatenate([key_flat, value_flat], axis=1)[None]
    block_ids = jnp.zeros((1,), jnp.int32)
    plane = nx * nlo
    piece = lax.all_to_all(
        jnp.broadcast_to(piece, (plane,) + piece.shape[1:]), ("x", "ylo"), 0, 0, tiled=True
    )
    block_ids = jnp.arange(plane, dtype=jnp.int32)
    back = -(--(-(max_len - 1) // tokens) // plane)
    piece, block_ids = ring_gather(piece, block_ids, "z", plane, lambda p, d: 1 <= d - p <= back)
    span = piece.shape[0] * tokens
    kv_all = piece.reshape(span, 2 * kv_cols)
    key_pos = (block_ids[:, None] * tokens + jnp.arange(tokens, dtype=jnp.int32)[None, :]).reshape(
        span
    )
    key_heads = kv_all[:, :kv_cols].reshape(span, kv_local, head_dim)
    value_heads = kv_all[:, kv_cols:].reshape(span, kv_local, head_dim)
    query_grid = queries.reshape(tokens, kv_local, group, head_dim)
    inv_root = 1.0 / math.sqrt(head_dim)
    score = (
        jnp.einsum("qhgd,khd->hgqk", query_grid, key_heads, preferred_element_type=jnp.float32)
        * inv_root
    )
    visible = (key_pos[None, :] >= seg_start[:, None]) & (key_pos[None, :] <= token_pos[:, None])
    score = jnp.where(visible[None, None], score, masked)
    top = jnp.max(score, axis=-1, keepdims=True)
    weights = jnp.where(visible[None, None], jnp.exp(score - top), 0.0)
    denom = jnp.sum(weights, axis=-1)
    summed = jnp.einsum(
        "hgqk,khd->hgqd",
        weights.astype(jnp.bfloat16),
        value_heads,
        preferred_element_type=jnp.float32,
    )
    attn = summed / denom[..., None]
    attn = jnp.transpose(attn, (2, 0, 1, 3)).reshape(tokens, q_cols).astype(jnp.bfloat16)
    part = jnp.dot(attn, w_out, preferred_element_type=jnp.float32).astype(jnp.bfloat16)
    nyhi = lax.axis_size("yhi")
    ncore = lax.axis_size("core")
    chunk = tokens // (nyhi * ncore)
    part = part.reshape(nyhi, ncore, chunk, -1).transpose(1, 0, 2, 3)
    part = lax.all_to_all(part, "core", 0, 0, tiled=True)
    part = jnp.sum(part.astype(jnp.float32), axis=0).astype(jnp.bfloat16)
    part = lax.all_to_all(part, "yhi", 0, 0, tiled=True)
    mixed = jnp.sum(part.astype(jnp.float32), axis=0).astype(jnp.bfloat16)
    return (mixed, key_flat, value_flat)


def solution(mesh):
    devices = mesh.devices
    nseq, nten = devices.shape
    nz = len({d.coords[2] for d in devices[:, 0]})
    nx = len({d.coords[0] for d in devices[:, 0]})
    ncore = len({d.core_on_chip for d in devices[0, :]})
    split = Mesh(devices.reshape(nz, nx, nseq // (nz * nx), nten // ncore, ncore), SEQ + TEN)
    seq, ten = (SEQ, TEN)
    placed = (
        P(seq, ten),
        P(),
        P(None, ten),
        P(None, ten),
        P(None, ten),
        P(ten, None),
        P(),
        P(),
        P(),
    )
    return jax.shard_map(
        on_device,
        mesh=split,
        in_specs=placed,
        out_specs=(P(seq + ten, None), P(seq, ten), P(seq, ten)),
        check_vma=False,
    )
```

profile of v0, /device:TPU:8, one launch (start us, length us, event | category | flops | bytes accessed | tf_op | source)
XLA Modules:
  0.0 132.9 jit_solution(4842833008063111337)
XLA Ops:
  0.6 0.0 copy-start
  0.7 17.5 %all_gather.3 = bf16[128,2560]{0,1:T(8,128)(2,1)S(1)} all-gather(bf16[128,320]{0,1:T(8,128)(2,1)} %param.9), channel_id=1, replica_groups=mesh['z'=8,'x'=4,'ylo'=2,'yhi'=4,'core'=2] {'yhi','core'}, dimensions={1}, use_global_device_ids=true | all-gather | bytes 737280 | tf_op jit(solution)/shard_map/all_gather | solution.py:117
  18.1 0.4 fusion.17
  18.5 3.1 %fusion.18 = f32[128,512]{1,0:T(8,128)S(1)} fusion(bf16[2560,128]{1,0:T(8,128)(2,1)} %param.13, bf16[2560,128]{1,0:T(8,128)(2,1)} %param.12, bf16[2560,256]{1,0:T(8,128)(2,1)} %param.11, bf16[128,2560]{0,1:T(8,128)(2,1)S(1)} %all_gather.3, f32[2560]{0:T(1024)} %param.10, f32[128]{0:T(128)S(1)} %add_rsqrt_fusion.2), kind=kOutput, calls=%fused_computation.25 | convolution fusion | flops 344457216 | bytes 3549696 | tf_op jit(solution)/shard_map/dot_general | solution.py:120
  21.6 0.0 copy-start.7
  21.6 0.1 multiply_reduce_fusion.1
  21.7 0.0 copy-start.5
  21.8 0.0 copy-done.8
  21.8 0.1 copy.32
  21.9 0.1 reduce.6
  22.0 0.1 convert_reduce_fusion
  22.1 0.1 select_reduce_fusion
  22.2 0.0 copy-done.6
  22.2 0.1 multiply_bitcast_fusion
  22.3 0.3 fusion.42
  22.6 0.0 copy-start.1
  22.6 0.0 copy-start.3
  22.7 0.1 pad_maximum_fusion
  22.8 0.8 broadcast_in_dim.31
  23.6 0.0 copy-done.1
  23.6 0.0 copy-done.3
  23.6 7.2 %all-to-all-start = ((bf16[8,128,256]{2,1,0:T(8,128)(2,1)}), bf16[8,128,256]{2,1,0:T(8,128)(2,1)S(1)}, u32[]{:S(2)}, u32[]{:S(2)}) async-start(bf16[8,128,256]{2,1,0:T(8,128)(2,1)} %broadcast_in_dim.31), calls=%async_computation | async-start | bytes 1048576 | tf_op jit(solution)/shard_map/all_to_all | solution.py:139
  30.8 0.0 copy-done.5
  31.0 0.1 slice_add_fusion
  31.1 0.1 concatenate.34
  31.1 0.1 add_bitcast_fusion
  31.2 0.7 reshape.365
  31.9 3.7 %compare_and_fusion = pred[128,8192]{0,1:T(8,128)(4,1)S(1)} fusion(s32[128]{0:T(128)S(1)} %iota_add_fusion, s32[128]{0:T(128)S(1)} %select_reduce_fusion, s32[8192]{0:T(1024)S(1)} %add_bitcast_fusion), kind=kLoop, calls=%fused_computation.11 | loop fusion | flops 3145728 | bytes 1082368 | tf_op jit(solution)/shard_map/and | solution.py:158
  35.7 4.9 %all-to-all-done = bf16[8,128,256]{2,1,0:T(8,128)(2,1)S(1)} async-done(((bf16[8,128,256]{2,1,0:T(8,128)(2,1)}), bf16[8,128,256]{2,1,0:T(8,128)(2,1)S(1)}, u32[]{:S(2)}, u32[]{:S(2)}) %all-to-all-start) | async-done | bytes 524320 | tf_op jit(solution)/shard_map/all_to_all | solution.py:139
  40.6 2.4 %collective-permute-start = (bf16[8,128,256]{2,1,0:T(8,128)(2,1)S(1)}, bf16[8,128,256]{2,1,0:T(8,128)(2,1)S(1)}, u32[]{:S(2)}, u32[]{:S(2)}) collective-permute-start(bf16[8,128,256]{2,1,0:T(8,128)(2,1)S(1)} %all-to-all-done), channel_id=1, source_target_pairs={{0,64},{64,128},{128,192},{192,256},{256,320},{320,384},{384,448},... | collective-permute-start | bytes 1572872 | tf_op jit(solution)/shard_map/ppermute | solution.py:82
  43.0 1.7 %multiply_reduce_fusion = f32[128,2]{1,0:T(8,128)} fusion(f32[128,2,128]{2,1,0:T(2,128)} %reshape.365), kind=kLoop, calls=%fused_computation.34 | loop fusion | flops 65280 | bytes 132096 | tf_op jit(solution)/shard_map/reduce_sum | solution.py:28
  44.7 0.9 copy.33
  45.6 8.3 %collective-permute-start.1 = (bf16[8,128,256]{2,1,0:T(8,128)(2,1)S(1)}, bf16[8,128,256]{2,1,0:T(8,128)(2,1)S(1)}, u32[]{:S(2)}, u32[]{:S(2)}) collective-permute-start(bf16[8,128,256]{2,1,0:T(8,128)(2,1)S(1)} %all-to-all-done), channel_id=1, source_target_pairs={{0,448},{64,0},{128,64},{192,128},{1,449},{65,1},{129,65},{193,129... | collective-permute-start | bytes 1572872 | tf_op jit(solution)/shard_map/ppermute | solution.py:83
  53.9 0.0 copy-done.7
  53.9 0.1 fusion.29
  54.0 0.0 collective-permute-done
  54.0 0.7 collective-permute-start.2
  54.7 0.3 multiply_cosine_fusion
  55.0 9.2 %collective-permute-done.1 = bf16[8,128,256]{2,1,0:T(8,128)(2,1)S(1)} collective-permute-done((bf16[8,128,256]{2,1,0:T(8,128)(2,1)S(1)}, bf16[8,128,256]{2,1,0:T(8,128)(2,1)S(1)}, u32[]{:S(2)}, u32[]{:S(2)}) %collective-permute-start.1) | collective-permute-done | bytes 524320 | tf_op jit(solution)/shard_map/ppermute | solution.py:83
  64.2 5.6 %collective-permute-start.3 = (bf16[8,128,256]{2,1,0:T(8,128)(2,1)S(1)}, bf16[8,128,256]{2,1,0:T(8,128)(2,1)S(1)}, u32[]{:S(2)}, u32[]{:S(2)}) collective-permute-start(bf16[8,128,256]{2,1,0:T(8,128)(2,1)S(1)} %collective-permute-done.1), channel_id=1, source_target_pairs={{0,448},{64,0},{128,64},{448,384},{1,449},{65,1},{129,65},{449,385... | collective-permute-start | bytes 1572872 | tf_op jit(solution)/shard_map/ppermute | solution.py:83
  69.8 0.1 subtract_convert_fusion
  70.0 0.0 collective-permute-done.2
  70.1 0.7 collective-permute-start.4
  70.7 0.7 collective-permute-start.6
  71.5 7.8 %collective-permute-done.3 = bf16[8,128,256]{2,1,0:T(8,128)(2,1)S(1)} collective-permute-done((bf16[8,128,256]{2,1,0:T(8,128)(2,1)S(1)}, bf16[8,128,256]{2,1,0:T(8,128)(2,1)S(1)}, u32[]{:S(2)}, u32[]{:S(2)}) %collective-permute-start.3) | collective-permute-done | bytes 524320 | tf_op jit(solution)/shard_map/ppermute | solution.py:83
  79.3 4.1 %collective-permute-start.5 = (bf16[4,128,256]{2,1,0:T(8,128)(2,1)S(1)}, bf16[4,128,256]{2,1,0:T(8,128)(2,1)S(1)}, u32[]{:S(2)}, u32[]{:S(2)}) collective-permute-start(bf16[4,128,256]{2,1,0:T(8,128)(2,1)S(1)} %slice.58), channel_id=1, source_target_pairs={{0,384},{64,448},{384,256},{448,320},{1,385},{65,449},{385,257},{4... | collective-permute-start | bytes 786440 | tf_op jit(solution)/shard_map/ppermute | solution.py:80
  83.5 3.9 %collective-permute-start.7 = (bf16[8,128,256]{2,1,0:T(8,128)(2,1)S(1)}, bf16[8,128,256]{2,1,0:T(8,128)(2,1)S(1)}, u32[]{:S(2)}, u32[]{:S(2)}) collective-permute-start(bf16[8,128,256]{2,1,0:T(8,128)(2,1)S(1)} %collective-permute-done.3), channel_id=1, source_target_pairs={{0,448},{64,0},{384,320},{448,384},{1,449},{65,1},{385,321},{449,3... | collective-permute-start | bytes 1572872 | tf_op jit(solution)/shard_map/ppermute | solution.py:83
  87.4 0.0 collective-permute-done.4
  87.4 7.1 %collective-permute-done.5 = bf16[4,128,256]{2,1,0:T(8,128)(2,1)S(1)} collective-permute-done((bf16[4,128,256]{2,1,0:T(8,128)(2,1)S(1)}, bf16[4,128,256]{2,1,0:T(8,128)(2,1)S(1)}, u32[]{:S(2)}, u32[]{:S(2)}) %collective-permute-start.5) | collective-permute-done | bytes 262176 | tf_op jit(solution)/shard_map/ppermute | solution.py:80
  94.6 0.0 collective-permute-done.6
  94.6 9.0 %collective-permute-done.7 = bf16[8,128,256]{2,1,0:T(8,128)(2,1)S(1)} collective-permute-done((bf16[8,128,256]{2,1,0:T(8,128)(2,1)S(1)}, bf16[8,128,256]{2,1,0:T(8,128)(2,1)S(1)}, u32[]{:S(2)}, u32[]{:S(2)}) %collective-permute-start.7) | collective-permute-done | bytes 524320 | tf_op jit(solution)/shard_map/ppermute | solution.py:83
  103.6 1.9 %fusion.47 = (f32[2,128]{1,0:T(2,128)S(1)}, f32[1,2,128,8192]{2,3,1,0:T(8,128)S(1)}) fusion(bf16[128,2,64]{2,0,1:T(8,128)(2,1)S(1)} %get-tuple-element.4, bf16[128,2,64]{2,0,1:T(8,128)(2,1)S(1)} %get-tuple-element.3, bf16[8192,256]{1,0:T(8,128)(2,1)S(1)} %bitcast.55, pred[128,8192]{0,1:T(8,128)(4,1)S(1)} %compare_and_fusion), kind=kOutput, calls=%fused_computation.91 | convolution fusion | flops 543293184 | bytes 11666432 | tf_op jit(solution)/shard_map/qhgd,khd->hgqk/dot_general | solution.py:155
  105.5 1.7 %fusion.2 = f32[2,128]{1,0:T(2,128)S(1)} fusion(f32[1,2,128,8192]{2,3,1,0:T(8,128)S(1)} %get-tuple-element.12, f32[2,128]{1,0:T(2,128)S(1)} %get-tuple-element.11, pred[128,8192]{0,1:T(8,128)(4,1)S(1)} %compare_and_fusion), kind=kLoop, calls=%fused_computation.4 | loop fusion | flops 6291200 | bytes 9439232 | tf_op jit(solution)/shard_map/reduce_sum | solution.py:162
  107.2 1.8 %fusion.24 = bf16[2,128,128]{1,2,0:T(8,128)(2,1)S(1)} fusion(bf16[8192,256]{1,0:T(8,128)(2,1)S(1)} %bitcast.56, f32[1,2,128,8192]{2,3,1,0:T(8,128)S(1)} %get-tuple-element.12, f32[2,128]{1,0:T(2,128)S(1)} %get-tuple-element.11, pred[128,8192]{0,1:T(8,128)(4,1)S(1)} %compare_and_fusion, f32[2,128]{1,0:T(2,128)S(1)} %fusion.2), kind=kOutput, calls=%fused_computation.27 | convolution fusion | flops 543227904 | bytes 11601920 | tf_op jit(solution)/shard_map/hgqk,khd->hgqd/dot_general | solution.py:163
  109.0 0.0 copy-start.2
  109.0 0.0 copy-start.4
  109.0 0.4 convolution_convert_fusion
  109.4 4.3 %all_to_all.15 = bf16[2,4,16,2560]{3,2,1,0:T(8,128)(2,1)S(1)} all-to-all(bf16[2,4,16,2560]{3,2,1,0:T(8,128)(2,1)S(1)} %bitcast.53), channel_id=1, replica_groups=mesh['z'=8,'x'=4,'ylo'=2,'yhi'=4,'core'=2] {'core'}, dimensions={0} | all-to-all | bytes 1310720 | tf_op jit(solution)/shard_map/all_to_all | solution.py:176
  113.7 0.9 reduce_sum.84
  114.6 4.6 %all-to-all-start.2 = ((bf16[4,16,2560]{2,1,0:T(8,128)(2,1)}), bf16[4,16,2560]{2,1,0:T(8,128)(2,1)S(1)}, u32[]{:S(2)}, u32[]{:S(2)}) async-start(bf16[4,16,2560]{2,1,0:T(8,128)(2,1)} %reduce_sum.84), calls=%async_computation.2 | async-start | bytes 655360 | tf_op jit(solution)/shard_map/all_to_all | solution.py:178
  119.2 0.0 copy-done.4
  119.2 0.7 pad_maximum_fusion.1
  119.9 12.3 %all-to-all-done.2 = bf16[4,16,2560]{2,1,0:T(8,128)(2,1)S(1)} async-done(((bf16[4,16,2560]{2,1,0:T(8,128)(2,1)}), bf16[4,16,2560]{2,1,0:T(8,128)(2,1)S(1)}, u32[]{:S(2)}, u32[]{:S(2)}) %all-to-all-start.2) | async-done | bytes 327712 | tf_op jit(solution)/shard_map/all_to_all | solution.py:178
  132.2 0.7 reduce_sum.85
  (33 shorter events, 0.5 us)
Async XLA Ops:
  0.6 108.4 %copy-start = (bf16[256,2560]{1,0:T(8,128)(2,1)S(1)}, bf16[256,2560]{1,0:T(8,128)(2,1)}, u32[]{:S(2)}) copy-start(bf16[256,2560]{1,0:T(8,128)(2,1)} %param.14) | copy-start | bytes 3932164
  18.1 3.6 %copy-start.8 = (s32[16]{0:T(128)S(1)}, s32[16]{0:T(128)}, u32[]{:S(2)}) copy-start(s32[16]{0:T(128)} %param.17) | copy-start | bytes 196
  18.1 4.1 %copy-start.6 = (f32[128]{0:T(128)S(1)}, f32[128]{0:T(128)}, u32[]{:S(2)}) copy-start(f32[128]{0:T(128)} %param.16) | copy-start | bytes 1540
  21.6 32.3 %copy-start.7 = (f32[128]{0:T(128)S(1)}, f32[128]{0:T(128)}, u32[]{:S(2)}) copy-start(f32[128]{0:T(128)} %param.15) | copy-start | bytes 1540
  21.7 9.1 %copy-start.5 = (bf16[128,128]{1,0:T(8,128)(2,1)}, bf16[128,128]{1,0:T(8,128)(2,1)S(1)}, u32[]{:S(2)}) copy-start(bf16[128,128]{1,0:T(8,128)(2,1)S(1)} %slice.94) | copy-start | bytes 98308
  22.6 0.9 copy-start.1
  22.6 0.9 copy-start.3
  23.6 17.0 %all-to-all-start = ((bf16[8,128,256]{2,1,0:T(8,128)(2,1)}), bf16[8,128,256]{2,1,0:T(8,128)(2,1)S(1)}, u32[]{:S(2)}, u32[]{:S(2)}) async-start(bf16[8,128,256]{2,1,0:T(8,128)(2,1)} %broadcast_in_dim.31), calls=%async_computation | async-start | bytes 1048576 | tf_op jit(solution)/shard_map/all_to_all | solution.py:139
  40.6 13.5 %collective-permute-start = (bf16[8,128,256]{2,1,0:T(8,128)(2,1)S(1)}, bf16[8,128,256]{2,1,0:T(8,128)(2,1)S(1)}, u32[]{:S(2)}, u32[]{:S(2)}) collective-permute-start(bf16[8,128,256]{2,1,0:T(8,128)(2,1)S(1)} %all-to-all-done), channel_id=1, source_target_pairs={{0,64},{64,128},{128,192},{192,256},{256,320},{320,384},{384,448},... | collective-permute-start | bytes 1572872 | tf_op jit(solution)/shard_map/ppermute | solution.py:82
  45.6 18.6 %collective-permute-start.1 = (bf16[8,128,256]{2,1,0:T(8,128)(2,1)S(1)}, bf16[8,128,256]{2,1,0:T(8,128)(2,1)S(1)}, u32[]{:S(2)}, u32[]{:S(2)}) collective-permute-start(bf16[8,128,256]{2,1,0:T(8,128)(2,1)S(1)} %all-to-all-done), channel_id=1, source_target_pairs={{0,448},{64,0},{128,64},{192,128},{1,449},{65,1},{129,65},{193,129... | collective-permute-start | bytes 1572872 | tf_op jit(solution)/shard_map/ppermute | solution.py:83
  54.0 16.0 %collective-permute-start.2 = (bf16[8,128,256]{2,1,0:T(8,128)(2,1)S(1)}, bf16[8,128,256]{2,1,0:T(8,128)(2,1)S(1)}, u32[]{:S(2)}, u32[]{:S(2)}) collective-permute-start(bf16[8,128,256]{2,1,0:T(8,128)(2,1)S(1)} %collective-permute-done), channel_id=1, source_target_pairs={{64,128},{128,192},{192,256},{256,320},{320,384},{384,448},{65,129... | collective-permute-start | bytes 1572872 | tf_op jit(solution)/shard_map/ppermute | solution.py:82
  64.2 15.1 %collective-permute-start.3 = (bf16[8,128,256]{2,1,0:T(8,128)(2,1)S(1)}, bf16[8,128,256]{2,1,0:T(8,128)(2,1)S(1)}, u32[]{:S(2)}, u32[]{:S(2)}) collective-permute-start(bf16[8,128,256]{2,1,0:T(8,128)(2,1)S(1)} %collective-permute-done.1), channel_id=1, source_target_pairs={{0,448},{64,0},{128,64},{448,384},{1,449},{65,1},{129,65},{449,385... | collective-permute-start | bytes 1572872 | tf_op jit(solution)/shard_map/ppermute | solution.py:83
  70.1 17.3 %collective-permute-start.4 = (bf16[4,128,256]{2,1,0:T(8,128)(2,1)S(1)}, bf16[4,128,256]{2,1,0:T(8,128)(2,1)S(1)}, u32[]{:S(2)}, u32[]{:S(2)}) collective-permute-start(bf16[4,128,256]{2,1,0:T(8,128)(2,1)S(1)} %slice.57), channel_id=1, source_target_pairs={{128,256},{192,320},{256,384},{320,448},{129,257},{193,321},{257,3... | collective-permute-start | bytes 786440 | tf_op jit(solution)/shard_map/ppermute | solution.py:72
  70.7 23.8 %collective-permute-start.6 = (bf16[8,128,256]{2,1,0:T(8,128)(2,1)S(1)}, bf16[8,128,256]{2,1,0:T(8,128)(2,1)S(1)}, u32[]{:S(2)}, u32[]{:S(2)}) collective-permute-start(bf16[8,128,256]{2,1,0:T(8,128)(2,1)S(1)} %collective-permute-done.2), channel_id=1, source_target_pairs={{128,192},{192,256},{256,320},{320,384},{384,448},{129,193},{193,2... | collective-permute-start | bytes 1572872 | tf_op jit(solution)/shard_map/ppermute | solution.py:82
  79.3 15.2 %collective-permute-start.5 = (bf16[4,128,256]{2,1,0:T(8,128)(2,1)S(1)}, bf16[4,128,256]{2,1,0:T(8,128)(2,1)S(1)}, u32[]{:S(2)}, u32[]{:S(2)}) collective-permute-start(bf16[4,128,256]{2,1,0:T(8,128)(2,1)S(1)} %slice.58), channel_id=1, source_target_pairs={{0,384},{64,448},{384,256},{448,320},{1,385},{65,449},{385,257},{4... | collective-permute-start | bytes 786440 | tf_op jit(solution)/shard_map/ppermute | solution.py:80
  83.5 20.1 %collective-permute-start.7 = (bf16[8,128,256]{2,1,0:T(8,128)(2,1)S(1)}, bf16[8,128,256]{2,1,0:T(8,128)(2,1)S(1)}, u32[]{:S(2)}, u32[]{:S(2)}) collective-permute-start(bf16[8,128,256]{2,1,0:T(8,128)(2,1)S(1)} %collective-permute-done.3), channel_id=1, source_target_pairs={{0,448},{64,0},{384,320},{448,384},{1,449},{65,1},{385,321},{449,3... | collective-permute-start | bytes 1572872 | tf_op jit(solution)/shard_map/ppermute | solution.py:83
  109.0 10.2 %copy-start.2 = (bf16[128,64]{1,0:T(8,128)(2,1)S(1)}, bf16[128,64]{1,0:T(8,128)(2,1)}, u32[]{:S(2)}) copy-start(bf16[128,64]{1,0:T(8,128)(2,1)} %copy-done.1) | copy-start | bytes 49156
  109.0 10.2 %copy-start.4 = (bf16[128,64]{1,0:T(8,128)(2,1)S(1)}, bf16[128,64]{1,0:T(8,128)(2,1)}, u32[]{:S(2)}) copy-start(bf16[128,64]{1,0:T(8,128)(2,1)} %copy-done.3) | copy-start | bytes 49156
  114.6 17.7 %all-to-all-start.2 = ((bf16[4,16,2560]{2,1,0:T(8,128)(2,1)}), bf16[4,16,2560]{2,1,0:T(8,128)(2,1)S(1)}, u32[]{:S(2)}, u32[]{:S(2)}) async-start(bf16[4,16,2560]{2,1,0:T(8,128)(2,1)} %reduce_sum.84), calls=%async_computation.2 | async-start | bytes 655360 | tf_op jit(solution)/shard_map/all_to_all | solution.py:178
where the time goes:
time: 134 us; the launch traced here: 133 us
  waiting for transfers between devices  50.3 us (38%)
  starting transfers between devices  38.2 us (29%)
  blocking collectives  21.7 us (16%)
  other arithmetic  11.4 us (9%)
  matrix products  7.1 us (5%)
  local copies, waits for them, and re-layouts  3.07 us (2%)
    ppermute x3, waiting for transfers between devices, ring_gather(): b = lax.ppermute(b, name, ring_pairs(n, s, False, needed))  26 us
    ppermute x3, starting transfers between devices, ring_gather(): b = lax.ppermute(b, name, ring_pairs(n, s, False, needed))  17.7 us
    all_gather x1, blocking collectives, on_device(): piece = lax.all_gather(hidden_in, TEN, axis=1, tiled=True)  17.5 us
    all_to_all x1, waiting for transfers between devices, on_device(): part = lax.all_to_all(part, 'yhi', 0, 0, tiled=True)  12.3 us
    all_to_all x1, starting transfers between devices, on_device(): lax.all_to_all(jnp.broadcast_to(piece, (plane,) + piece.shape[1:]), ('x',...  7.23 us
    ppermute x1, waiting for transfers between devices, ring_gather(): pieces.append(lax.ppermute(b[half:], name, behind))  7.1 us
    all_to_all x1, waiting for transfers between devices, on_device(): lax.all_to_all(jnp.broadcast_to(piece, (plane,) + piece.shape[1:]), ('x',...  4.9 us
    all_to_all x1, starting transfers between devices, on_device(): part = lax.all_to_all(part, 'yhi', 0, 0, tiled=True)  4.64 us
  transfers between devices with their start and end apart: 10, of which 6 were waited for; matrix products, arithmetic and copies ran while one was open for 7% of the time, Pallas kernels for 0%

commit v1 on v0

--- a/solution.py
+++ b/solution.py
@@ -114,7 +114,9 @@
     kv_local = kv_cols // head_dim
     group = q_cols // kv_cols
     combined = jnp.concatenate([w_query, w_key, w_value], axis=1)
-    piece = lax.all_gather(hidden_in, TEN, axis=1, tiled=True)
+    piece = jnp.concatenate(
+        lax.all_to_all(jnp.stack([hidden_in] * lax.axis_size(TEN)), TEN, 0, 0), axis=1
+    )
     wide = piece.astype(jnp.float32)
     scaled = (wide * norm_gain[None, :]).astype(jnp.bfloat16)
     acc = jnp.dot(scaled, combined, preferred_element_type=jnp.float32)

time: 134 us -> 138 us (1.030)
  the two profiles are of different devices: /device:TPU:8 before, /device:TPU:17 now
where the time goes in v1:
time: 138 us; the launch traced here: 137 us
  waiting for transfers between devices  55.1 us (40%)
  starting transfers between devices  47.3 us (34%)
  other arithmetic  14.7 us (11%)
  local copies, waits for them, and re-layouts  6.7 us (5%)
  blocking collectives  6.29 us (5%)
  matrix products  6.1 us (4%)
    ppermute x3, waiting for transfers between devices, ring_gather(): b = lax.ppermute(b, name, ring_pairs(n, s, False, needed))  23 us
    ppermute x3, starting transfers between devices, ring_gather(): b = lax.ppermute(b, name, ring_pairs(n, s, False, needed))  16.2 us
    all_to_all x1, waiting for transfers between devices, on_device(): lax.all_to_all(jnp.stack([hidden_in] * lax.axis_size(TEN)), TEN, 0, 0)  13.9 us
    all_to_all x1, waiting for transfers between devices, on_device(): part = lax.all_to_all(part, 'yhi', 0, 0, tiled=True)  10.4 us
    all_to_all x1, starting transfers between devices, on_device(): lax.all_to_all(jnp.stack([hidden_in] * lax.axis_size(TEN)), TEN, 0, 0)  9.42 us
    all_to_all x1, blocking collectives, on_device(): part = lax.all_to_all(part, 'core', 0, 0, tiled=True)  6.29 us
    ppermute x3, starting transfers between devices, ring_gather(): a = lax.ppermute(a, name, ring_pairs(n, s, True, needed))  6.17 us
    ppermute x1, starting transfers between devices, ring_gather(): pieces.append(lax.ppermute(b[half:], name, behind))  5.67 us
  transfers between devices with their start and end apart: 11, of which 7 were waited for; matrix products, arithmetic and copies ran while one was open for 10% of the time, Pallas kernels for 0%

profile of v1, /device:TPU:17, one launch (start us, length us, event | category | flops | bytes accessed | tf_op | source)
XLA Modules:
  0.0 137.2 jit_solution(1110182268932040493)
XLA Ops:
  0.6 0.0 copy-start
  0.6 0.0 copy-start.8
  0.7 1.9 %stack.2 = bf16[8,128,320]{1,2,0:T(8,128)(2,1)} broadcast(bf16[128,320]{0,1:T(8,128)(2,1)} %param.9), dimensions={1,2} | broadcast | bytes 737280 | tf_op jit(solution)/shard_map/stack | solution.py:118
  2.6 9.4 %all-to-all-start = ((bf16[8,128,320]{1,2,0:T(8,128)(2,1)}), bf16[8,128,320]{1,2,0:T(8,128)(2,1)S(1)}, u32[]{:S(2)}, u32[]{:S(2)}) async-start(bf16[8,128,320]{1,2,0:T(8,128)(2,1)} %stack.2), calls=%async_computation | async-start | bytes 1310720 | tf_op jit(solution)/shard_map/all_to_all | solution.py:118
  12.1 0.1 slice_add_fusion
  12.1 0.7 copy.33
  12.9 0.1 reduce.8
  13.0 0.7 sub.36
  13.7 0.1 concatenate.34
  13.8 0.1 convert_reduce_fusion
  13.9 0.1 select_reduce_fusion
  14.0 0.1 add_bitcast_fusion
  14.1 13.9 %all-to-all-done = bf16[8,128,320]{1,2,0:T(8,128)(2,1)S(1)} async-done(((bf16[8,128,320]{1,2,0:T(8,128)(2,1)}), bf16[8,128,320]{1,2,0:T(8,128)(2,1)S(1)}, u32[]{:S(2)}, u32[]{:S(2)}) %all-to-all-start) | async-done | bytes 655392 | tf_op jit(solution)/shard_map/all_to_all | solution.py:118
  27.9 0.4 multiply_reduce_fusion
  28.3 1.1 fusion.16
  29.4 0.0 copy-start.7
  29.4 2.1 %fusion.17 = f32[128,512]{1,0:T(8,128)S(1)} fusion(bf16[128,2560]{0,1:T(8,128)(2,1)S(1)} %fusion.16, bf16[2560,128]{1,0:T(8,128)(2,1)S(1)} %copy-done.8, bf16[2560,128]{1,0:T(8,128)(2,1)} %param.12, bf16[2560,256]{1,0:T(8,128)(2,1)} %param.11, f32[128]{0:T(128)S(1)} %add_rsqrt_fusion.2), kind=kOutput, calls=%fused_computation.24 | convolution fusion | flops 343474176 | bytes 3539456 | tf_op jit(solution)/shard_map/dot_general | solution.py:122
  31.5 0.1 multiply_reduce_fusion.2
  31.7 0.0 copy-start.5
  31.7 0.1 multiply_bitcast_fusion
  31.8 0.3 fusion.39
  32.1 0.0 copy-start.3
  32.1 0.1 pad_maximum_fusion
  32.2 0.8 broadcast_in_dim.31
  33.1 0.0 copy-done.5
  33.1 4.4 %all-to-all-start.1 = ((bf16[8,128,256]{2,1,0:T(8,128)(2,1)}), bf16[8,128,256]{2,1,0:T(8,128)(2,1)S(1)}, u32[]{:S(2)}, u32[]{:S(2)}) async-start(bf16[8,128,256]{2,1,0:T(8,128)(2,1)} %broadcast_in_dim.31), calls=%async_computation.1 | async-start | bytes 1048576 | tf_op jit(solution)/shard_map/all_to_all | solution.py:141
  37.4 3.7 %compare_and_fusion = pred[128,8192]{0,1:T(8,128)(4,1)S(1)} fusion(s32[128]{0:T(128)S(1)} %iota_add_fusion, s32[128]{0:T(128)S(1)} %select_reduce_fusion, s32[8192]{0:T(1024)S(1)} %add_bitcast_fusion), kind=kLoop, calls=%fused_computation.11 | loop fusion | flops 3145728 | bytes 1082368 | tf_op jit(solution)/shard_map/and | solution.py:160
  41.1 0.9 multiply_cosine_fusion
  42.1 4.0 %all-to-all-done.1 = bf16[8,128,256]{2,1,0:T(8,128)(2,1)S(1)} async-done(((bf16[8,128,256]{2,1,0:T(8,128)(2,1)}), bf16[8,128,256]{2,1,0:T(8,128)(2,1)S(1)}, u32[]{:S(2)}, u32[]{:S(2)}) %all-to-all-start.1) | async-done | bytes 524320 | tf_op jit(solution)/shard_map/all_to_all | solution.py:141
  46.1 4.8 %collective-permute-start = (bf16[8,128,256]{2,1,0:T(8,128)(2,1)S(1)}, bf16[8,128,256]{2,1,0:T(8,128)(2,1)}, u32[]{:S(2)}, u32[]{:S(2)}) collective-permute-start(bf16[8,128,256]{2,1,0:T(8,128)(2,1)S(1)} %all-to-all-done.1), channel_id=1, source_target_pairs={{0,64},{64,128},{128,192},{192,256},{256,320},{320,384},{384,448},... | collective-permute-start | bytes 1572872 | tf_op jit(solution)/shard_map/ppermute | solution.py:82
  50.9 0.7 reshape.371
  51.6 7.2 %collective-permute-start.1 = (bf16[8,128,256]{2,1,0:T(8,128)(2,1)S(1)}, bf16[8,128,256]{2,1,0:T(8,128)(2,1)S(1)}, u32[]{:S(2)}, u32[]{:S(2)}) collective-permute-start(bf16[8,128,256]{2,1,0:T(8,128)(2,1)S(1)} %all-to-all-done.1), channel_id=1, source_target_pairs={{0,448},{64,0},{128,64},{192,128},{1,449},{65,1},{129,65},{193,129... | collective-permute-start | bytes 1572872 | tf_op jit(solution)/shard_map/ppermute | solution.py:83
  58.8 1.7 %multiply_reduce_fusion.1 = f32[128,2]{1,0:T(8,128)} fusion(f32[128,2,128]{2,1,0:T(2,128)} %reshape.371), kind=kLoop, calls=%fused_computation.32 | loop fusion | flops 65280 | bytes 132096 | tf_op jit(solution)/shard_map/reduce_sum | solution.py:28
  60.5 0.9 copy.34
  61.4 0.0 collective-permute-done
  61.5 0.7 collective-permute-start.2
  62.2 0.1 fusion.26
  62.3 5.4 %collective-permute-done.1 = bf16[8,128,256]{2,1,0:T(8,128)(2,1)S(1)} collective-permute-done((bf16[8,128,256]{2,1,0:T(8,128)(2,1)S(1)}, bf16[8,128,256]{2,1,0:T(8,128)(2,1)S(1)}, u32[]{:S(2)}, u32[]{:S(2)}) %collective-permute-start.1) | collective-permute-done | bytes 524320 | tf_op jit(solution)/shard_map/ppermute | solution.py:83
  67.7 5.3 %collective-permute-start.3 = (bf16[8,128,256]{2,1,0:T(8,128)(2,1)S(1)}, bf16[8,128,256]{2,1,0:T(8,128)(2,1)S(1)}, u32[]{:S(2)}, u32[]{:S(2)}) collective-permute-start(bf16[8,128,256]{2,1,0:T(8,128)(2,1)S(1)} %collective-permute-done.1), channel_id=1, source_target_pairs={{0,448},{64,0},{128,64},{448,384},{1,449},{65,1},{129,65},{449,385... | collective-permute-start | bytes 1572872 | tf_op jit(solution)/shard_map/ppermute | solution.py:83
  73.0 1.0 subtract_convert_fusion
  74.0 1.1 constant_dynamic-update-slice_fusion.7
  75.1 0.0 collective-permute-done.2
  75.1 0.7 collective-permute-start.4
  75.8 0.7 collective-permute-start.6
  76.6 4.5 %collective-permute-done.3 = bf16[8,128,256]{2,1,0:T(8,128)(2,1)S(1)} collective-permute-done((bf16[8,128,256]{2,1,0:T(8,128)(2,1)S(1)}, bf16[8,128,256]{2,1,0:T(8,128)(2,1)S(1)}, u32[]{:S(2)}, u32[]{:S(2)}) %collective-permute-start.3) | collective-permute-done | bytes 524320 | tf_op jit(solution)/shard_map/ppermute | solution.py:83
  81.1 5.7 %collective-permute-start.5 = (bf16[4,128,256]{2,1,0:T(8,128)(2,1)S(1)}, bf16[4,128,256]{2,1,0:T(8,128)(2,1)S(1)}, u32[]{:S(2)}, u32[]{:S(2)}) collective-permute-start(bf16[4,128,256]{2,1,0:T(8,128)(2,1)S(1)} %slice.58), channel_id=1, source_target_pairs={{0,384},{64,448},{384,256},{448,320},{1,385},{65,449},{385,257},{4... | collective-permute-start | bytes 786440 | tf_op jit(solution)/shard_map/ppermute | solution.py:80
  86.7 3.7 %collective-permute-start.7 = (bf16[8,128,256]{2,1,0:T(8,128)(2,1)S(1)}, bf16[8,128,256]{2,1,0:T(8,128)(2,1)S(1)}, u32[]{:S(2)}, u32[]{:S(2)}) collective-permute-start(bf16[8,128,256]{2,1,0:T(8,128)(2,1)S(1)} %collective-permute-done.3), channel_id=1, source_target_pairs={{0,448},{64,0},{384,320},{448,384},{1,449},{65,1},{385,321},{449,3... | collective-permute-start | bytes 1572872 | tf_op jit(solution)/shard_map/ppermute | solution.py:83
  90.5 0.0 collective-permute-done.4
  90.6 3.9 %collective-permute-done.5 = bf16[4,128,256]{2,1,0:T(8,128)(2,1)S(1)} collective-permute-done((bf16[4,128,256]{2,1,0:T(8,128)(2,1)S(1)}, bf16[4,128,256]{2,1,0:T(8,128)(2,1)S(1)}, u32[]{:S(2)}, u32[]{:S(2)}) %collective-permute-start.5) | collective-permute-done | bytes 262176 | tf_op jit(solution)/shard_map/ppermute | solution.py:80
  94.5 0.0 collective-permute-done.6
  94.5 13.2 %collective-permute-done.7 = bf16[8,128,256]{2,1,0:T(8,128)(2,1)S(1)} collective-permute-done((bf16[8,128,256]{2,1,0:T(8,128)(2,1)S(1)}, bf16[8,128,256]{2,1,0:T(8,128)(2,1)S(1)}, u32[]{:S(2)}, u32[]{:S(2)}) %collective-permute-start.7) | collective-permute-done | bytes 524320 | tf_op jit(solution)/shard_map/ppermute | solution.py:83
  107.7 1.9 %fusion.44 = (f32[2,128]{1,0:T(2,128)S(1)}, f32[1,2,128,8192]{2,3,1,0:T(8,128)S(1)}) fusion(bf16[128,2,64]{2,0,1:T(8,128)(2,1)S(1)} %get-tuple-element.4, bf16[128,2,64]{2,0,1:T(8,128)(2,1)S(1)} %get-tuple-element.3, bf16[8192,256]{1,0:T(8,128)(2,1)S(1)} %bitcast.62, pred[128,8192]{0,1:T(8,128)(4,1)S(1)} %compare_and_fusion), kind=kOutput, calls=%fused_computation.89 | convolution fusion | flops 543293184 | bytes 11666432 | tf_op jit(solution)/shard_map/qhgd,khd->hgqk/dot_general | solution.py:157
  109.6 1.7 %fusion.2 = f32[2,128]{1,0:T(2,128)S(1)} fusion(f32[1,2,128,8192]{2,3,1,0:T(8,128)S(1)} %get-tuple-element.12, f32[2,128]{1,0:T(2,128)S(1)} %get-tuple-element.11, pred[128,8192]{0,1:T(8,128)(4,1)S(1)} %compare_and_fusion), kind=kLoop, calls=%fused_computation.4 | loop fusion | flops 6291200 | bytes 9439232 | tf_op jit(solution)/shard_map/reduce_sum | solution.py:164
  111.3 1.8 %fusion.23 = bf16[2,128,128]{1,2,0:T(8,128)(2,1)S(1)} fusion(bf16[8192,256]{1,0:T(8,128)(2,1)S(1)} %bitcast.63, f32[1,2,128,8192]{2,3,1,0:T(8,128)S(1)} %get-tuple-element.12, f32[2,128]{1,0:T(2,128)S(1)} %get-tuple-element.11, pred[128,8192]{0,1:T(8,128)(4,1)S(1)} %compare_and_fusion, f32[2,128]{1,0:T(2,128)S(1)} %fusion.2), kind=kOutput, calls=%fused_computation.26 | convolution fusion | flops 543227904 | bytes 11601920 | tf_op jit(solution)/shard_map/hgqk,khd->hgqd/dot_general | solution.py:165
  113.1 0.0 copy-start.4
  113.1 0.0 copy-done
  113.1 0.4 convolution_convert_fusion
  113.5 6.3 %all_to_all.20 = bf16[2,4,16,2560]{3,2,1,0:T(8,128)(2,1)S(1)} all-to-all(bf16[2,4,16,2560]{3,2,1,0:T(8,128)(2,1)S(1)} %bitcast.60), channel_id=1, replica_groups=mesh['z'=8,'x'=4,'ylo'=2,'yhi'=4,'core'=2] {'core'}, dimensions={0} | all-to-all | bytes 1310720 | tf_op jit(solution)/shard_map/all_to_all | solution.py:178
  119.8 0.9 reduce_sum.84
  120.7 4.8 %all-to-all-start.3 = ((bf16[4,16,2560]{2,1,0:T(8,128)(2,1)}), bf16[4,16,2560]{2,1,0:T(8,128)(2,1)S(1)}, u32[]{:S(2)}, u32[]{:S(2)}) async-start(bf16[4,16,2560]{2,1,0:T(8,128)(2,1)} %reduce_sum.84), calls=%async_computation.3 | async-start | bytes 655360 | tf_op jit(solution)/shard_map/all_to_all | solution.py:180
  125.5 0.0 copy-done.2
  125.5 0.7 pad_maximum_fusion.1
  126.2 10.4 %all-to-all-done.3 = bf16[4,16,2560]{2,1,0:T(8,128)(2,1)S(1)} async-done(((bf16[4,16,2560]{2,1,0:T(8,128)(2,1)}), bf16[4,16,2560]{2,1,0:T(8,128)(2,1)S(1)}, u32[]{:S(2)}, u32[]{:S(2)}) %all-to-all-start.3) | async-done | bytes 327712 | tf_op jit(solution)/shard_map/all_to_all | solution.py:180
  136.6 0.7 reduce_sum.85
  (36 shorter events, 0.5 us)
Async XLA Ops:
  0.6 112.5 %copy-start = (bf16[256,2560]{1,0:T(8,128)(2,1)S(1)}, bf16[256,2560]{1,0:T(8,128)(2,1)}, u32[]{:S(2)}) copy-start(bf16[256,2560]{1,0:T(8,128)(2,1)} %param.14) | copy-start | bytes 3932164
  0.6 28.8 %copy-start.8 = (bf16[2560,128]{1,0:T(8,128)(2,1)S(1)}, bf16[2560,128]{1,0:T(8,128)(2,1)}, u32[]{:S(2)}) copy-start(bf16[2560,128]{1,0:T(8,128)(2,1)} %param.13) | copy-start | bytes 1966084
  2.6 25.3 %all-to-all-start = ((bf16[8,128,320]{1,2,0:T(8,128)(2,1)}), bf16[8,128,320]{1,2,0:T(8,128)(2,1)S(1)}, u32[]{:S(2)}, u32[]{:S(2)}) async-start(bf16[8,128,320]{1,2,0:T(8,128)(2,1)} %stack.2), calls=%async_computation | async-start | bytes 1310720 | tf_op jit(solution)/shard_map/all_to_all | solution.py:118
  28.3 3.4 %copy-start.6 = (f32[128]{0:T(128)S(1)}, f32[128]{0:T(128)}, u32[]{:S(2)}) copy-start(f32[128]{0:T(128)} %param.16) | copy-start | bytes 1540
  29.4 32.7 %copy-start.7 = (f32[128]{0:T(128)S(1)}, f32[128]{0:T(128)}, u32[]{:S(2)}) copy-start(f32[128]{0:T(128)} %param.15) | copy-start | bytes 1540
  31.7 1.4 %copy-start.5 = (bf16[128,128]{1,0:T(8,128)(2,1)}, bf16[128,128]{1,0:T(8,128)(2,1)S(1)}, u32[]{:S(2)}) copy-start(bf16[128,128]{1,0:T(8,128)(2,1)S(1)} %slice.94) | copy-start | bytes 98308
  32.1 0.9 copy-start.1
  32.1 0.9 copy-start.3
  33.1 13.0 %all-to-all-start.1 = ((bf16[8,128,256]{2,1,0:T(8,128)(2,1)}), bf16[8,128,256]{2,1,0:T(8,128)(2,1)S(1)}, u32[]{:S(2)}, u32[]{:S(2)}) async-start(bf16[8,128,256]{2,1,0:T(8,128)(2,1)} %broadcast_in_dim.31), calls=%async_computation.1 | async-start | bytes 1048576 | tf_op jit(solution)/shard_map/all_to_all | solution.py:141
  46.1 15.4 %collective-permute-start = (bf16[8,128,256]{2,1,0:T(8,128)(2,1)S(1)}, bf16[8,128,256]{2,1,0:T(8,128)(2,1)}, u32[]{:S(2)}, u32[]{:S(2)}) collective-permute-start(bf16[8,128,256]{2,1,0:T(8,128)(2,1)S(1)} %all-to-all-done.1), channel_id=1, source_target_pairs={{0,64},{64,128},{128,192},{192,256},{256,320},{320,384},{384,448},... | collective-permute-start | bytes 1572872 | tf_op jit(solution)/shard_map/ppermute | solution.py:82
  51.6 16.1 %collective-permute-start.1 = (bf16[8,128,256]{2,1,0:T(8,128)(2,1)S(1)}, bf16[8,128,256]{2,1,0:T(8,128)(2,1)S(1)}, u32[]{:S(2)}, u32[]{:S(2)}) collective-permute-start(bf16[8,128,256]{2,1,0:T(8,128)(2,1)S(1)} %all-to-all-done.1), channel_id=1, source_target_pairs={{0,448},{64,0},{128,64},{192,128},{1,449},{65,1},{129,65},{193,129... | collective-permute-start | bytes 1572872 | tf_op jit(solution)/shard_map/ppermute | solution.py:83
  61.5 13.6 %collective-permute-start.2 = (bf16[8,128,256]{2,1,0:T(8,128)(2,1)}, bf16[8,128,256]{2,1,0:T(8,128)(2,1)S(1)}, u32[]{:S(2)}, u32[]{:S(2)}) collective-permute-start(bf16[8,128,256]{2,1,0:T(8,128)(2,1)} %collective-permute-done), channel_id=1, source_target_pairs={{64,128},{128,192},{192,256},{256,320},{320,384},{384,448},{65,129... | collective-permute-start | bytes 1572872 | tf_op jit(solution)/shard_map/ppermute | solution.py:82
  67.7 13.3 %collective-permute-start.3 = (bf16[8,128,256]{2,1,0:T(8,128)(2,1)S(1)}, bf16[8,128,256]{2,1,0:T(8,128)(2,1)S(1)}, u32[]{:S(2)}, u32[]{:S(2)}) collective-permute-start(bf16[8,128,256]{2,1,0:T(8,128)(2,1)S(1)} %collective-permute-done.1), channel_id=1, source_target_pairs={{0,448},{64,0},{128,64},{448,384},{1,449},{65,1},{129,65},{449,385... | collective-permute-start | bytes 1572872 | tf_op jit(solution)/shard_map/ppermute | solution.py:83
  75.1 15.4 %collective-permute-start.4 = (bf16[4,128,256]{2,1,0:T(8,128)(2,1)S(1)}, bf16[4,128,256]{2,1,0:T(8,128)(2,1)S(1)}, u32[]{:S(2)}, u32[]{:S(2)}) collective-permute-start(bf16[4,128,256]{2,1,0:T(8,128)(2,1)S(1)} %slice.57), channel_id=1, source_target_pairs={{128,256},{192,320},{256,384},{320,448},{129,257},{193,321},{257,3... | collective-permute-start | bytes 786440 | tf_op jit(solution)/shard_map/ppermute | solution.py:72
  75.8 18.6 %collective-permute-start.6 = (bf16[8,128,256]{2,1,0:T(8,128)(2,1)S(1)}, bf16[8,128,256]{2,1,0:T(8,128)(2,1)S(1)}, u32[]{:S(2)}, u32[]{:S(2)}) collective-permute-start(bf16[8,128,256]{2,1,0:T(8,128)(2,1)S(1)} %collective-permute-done.2), channel_id=1, source_target_pairs={{128,192},{192,256},{256,320},{320,384},{384,448},{129,193},{193,2... | collective-permute-start | bytes 1572872 | tf_op jit(solution)/shard_map/ppermute | solution.py:82
  81.1 13.4 %collective-permute-start.5 = (bf16[4,128,256]{2,1,0:T(8,128)(2,1)S(1)}, bf16[4,128,256]{2,1,0:T(8,128)(2,1)S(1)}, u32[]{:S(2)}, u32[]{:S(2)}) collective-permute-start(bf16[4,128,256]{2,1,0:T(8,128)(2,1)S(1)} %slice.58), channel_id=1, source_target_pairs={{0,384},{64,448},{384,256},{448,320},{1,385},{65,449},{385,257},{4... | collective-permute-start | bytes 786440 | tf_op jit(solution)/shard_map/ppermute | solution.py:80
  86.7 20.9 %collective-permute-start.7 = (bf16[8,128,256]{2,1,0:T(8,128)(2,1)S(1)}, bf16[8,128,256]{2,1,0:T(8,128)(2,1)S(1)}, u32[]{:S(2)}, u32[]{:S(2)}) collective-permute-start(bf16[8,128,256]{2,1,0:T(8,128)(2,1)S(1)} %collective-permute-done.3), channel_id=1, source_target_pairs={{0,448},{64,0},{384,320},{448,384},{1,449},{65,1},{385,321},{449,3... | collective-permute-start | bytes 1572872 | tf_op jit(solution)/shard_map/ppermute | solution.py:83
  113.1 12.4 %copy-start.2 = (bf16[128,64]{1,0:T(8,128)(2,1)S(1)}, bf16[128,64]{1,0:T(8,128)(2,1)}, u32[]{:S(2)}) copy-start(bf16[128,64]{1,0:T(8,128)(2,1)} %copy-done.1) | copy-start | bytes 49156
  113.1 12.4 %copy-start.4 = (bf16[128,64]{1,0:T(8,128)(2,1)S(1)}, bf16[128,64]{1,0:T(8,128)(2,1)}, u32[]{:S(2)}) copy-start(bf16[128,64]{1,0:T(8,128)(2,1)} %copy-done.3) | copy-start | bytes 49156
  120.7 15.9 %all-to-all-start.3 = ((bf16[4,16,2560]{2,1,0:T(8,128)(2,1)}), bf16[4,16,2560]{2,1,0:T(8,128)(2,1)S(1)}, u32[]{:S(2)}, u32[]{:S(2)}) async-start(bf16[4,16,2560]{2,1,0:T(8,128)(2,1)} %reduce_sum.84), calls=%async_computation.3 | async-start | bytes 655360 | tf_op jit(solution)/shard_map/all_to_all | solution.py:180
